TPU v7x, 128 devices: a whole 4x4x4 slice. The times are simulated.
128 devices in a mesh: rep: 64 (over z, y, x_hi, core), shard: 2 (over x_lo).
Axes of the slice: x: 4 (x_hi: 2, x_lo: 2; x = x_hi * 2 + x_lo), y: 4, z: 4, core: 2. Of those that a mesh axis runs over, the one named last changes fastest.
Arguments:
- grad_xproj: bfloat16 [256, 2, 3072, 128], P(('rep', 'shard')), may hold values from -32 to 32
- grad_chan: bfloat16 [256, 2, 118, 3072], P(('rep', 'shard')), may hold values from -32 to 32
- grad_embed: bfloat16 [256, 1024, 1536], P(('rep', 'shard')), may hold values from -32 to 32
- weight_xproj: float32 [2, 3072, 128], P(None, 'shard'), may hold values from -0.3125 to 0.3125
- weight_chan: float32 [2, 118, 3072], P(None, None, 'shard'), may hold values from -0.3125 to 0.3125
- weight_embed: float32 [1024, 1536], P('shard'), may hold values from -0.3125 to 0.3125
- moment_xproj: float32 [2, 3072, 128], P(None, 'shard'), may hold values from -0.015625 to 0.015625
- moment_chan: float32 [2, 118, 3072], P(None, None, 'shard'), may hold values from -0.015625 to 0.015625
- moment_embed: float32 [1024, 1536], P('shard'), may hold values from -0.015625 to 0.015625
- second_xproj: float32 [2, 3072, 128], P(None, 'shard'), may hold values from 1e-08 to 1e-05
- second_chan: float32 [2, 118, 3072], P(None, None, 'shard'), may hold values from 1e-08 to 1e-05
- second_embed: float32 [1024, 1536], P('shard'), may hold values from 1e-08 to 1e-05
Outputs:
- new_weight_xproj: float32 [2, 3072, 128], P(None, 'shard')
- new_weight_chan: float32 [2, 118, 3072], P(None, None, 'shard')
- new_weight_embed: float32 [1024, 1536], P('shard')
- new_moment_xproj: float32 [2, 3072, 128], P(None, 'shard')
- new_moment_chan: float32 [2, 118, 3072], P(None, None, 'shard')
- new_moment_embed: float32 [1024, 1536], P('shard')
- new_second_xproj: float32 [2, 3072, 128], P(None, 'shard')
- new_second_chan: float32 [2, 118, 3072], P(None, None, 'shard')
- new_second_embed: float32 [1024, 1536], P('shard')
- full_xproj: bfloat16 [2, 3072, 128], replicated
- full_chan: bfloat16 [2, 118, 3072], replicated
- full_embed: bfloat16 [1024, 1536], replicated
- pre_norm: float32 [1], replicated
All inputs are finite; a program needn't handle non-finite values.
Results may differ from a plain program's by a relative error of at most 0.00085.
Values may be sent and summed in bfloat16 or wider, within the bound.
No kernel may reach another device: no remote copies, remote signals or barrier semaphores. Data moves between devices by JAX's collectives and lax.ppermute only.
A program may use at most 448 MiB of HBM per device.

v0:
```python
import jax
import jax.numpy as jnp
from jax import lax
from jax.sharding import PartitionSpec as P

beta_one = 0.9
beta_two = 0.999
learn_rate = 0.003
decay_rate = 0.1
epsilon = 1e-08
correct_one = 0.9999734386011124
correct_two = 0.09520785288629094


def adamw_update(weight, moment, second, gradient, clip_factor):
    clipped = clip_factor * gradient
    new_moment = beta_one * moment + (1.0 - beta_one) * clipped
    new_second = beta_two * second + (1.0 - beta_two) * clipped * clipped
    step_size = new_moment / correct_one / (jnp.sqrt(new_second / correct_two) + epsilon)
    new_weight = weight - learn_rate * (step_size + decay_rate * weight)
    return (new_weight, new_moment, new_second)


def on_device(
    grad_xproj,
    grad_chan,
    grad_embed,
    weight_xproj,
    weight_chan,
    weight_embed,
    moment_xproj,
    moment_chan,
    moment_embed,
    second_xproj,
    second_chan,
    second_embed,
):
    count_rep = lax.axis_size("rep")
    count_shard = lax.axis_size("shard")
    micro, layers, inner, xw = grad_xproj.shape
    _, _, ch, _ = grad_chan.shape
    gx = grad_xproj.reshape(micro, layers, count_shard, inner // count_shard, xw)
    summed_x = jnp.transpose(jnp.sum(gx, axis=0, dtype=jnp.float32), (1, 0, 2, 3))
    gc = grad_chan.reshape(micro, layers, ch, count_shard, inner // count_shard)
    summed_c = jnp.transpose(jnp.sum(gc, axis=0, dtype=jnp.float32), (2, 0, 1, 3))
    summed_e = jnp.sum(grad_embed, axis=0, dtype=jnp.float32)
    part_x = lax.psum_scatter(
        summed_x.astype(jnp.bfloat16), "shard", scatter_dimension=0, tiled=True
    )
    part_c = lax.psum_scatter(
        summed_c.astype(jnp.bfloat16), "shard", scatter_dimension=0, tiled=True
    )
    part_e = lax.psum_scatter(
        summed_e.astype(jnp.bfloat16), "shard", scatter_dimension=0, tiled=True
    )
    block_x = lax.psum(part_x, "rep")[0]
    block_c = lax.psum(part_c, "rep")[0]
    block_e = lax.psum(part_e, "rep")
    inverse = 1.0 / (micro * count_rep * count_shard)
    mean_x = block_x.astype(jnp.float32) * inverse
    mean_c = block_c.astype(jnp.float32) * inverse
    mean_e = block_e.astype(jnp.float32) * inverse
    partial_squares = jnp.sum(mean_x * mean_x) + jnp.sum(mean_c * mean_c) + jnp.sum(mean_e * mean_e)
    squares = lax.psum(partial_squares, "shard")
    norm_value = jnp.sqrt(squares)
    clip_factor = jnp.minimum(1.0, 1.0 / (norm_value + 1e-06))
    wx, mx, vx = adamw_update(weight_xproj, moment_xproj, second_xproj, mean_x, clip_factor)
    wc, mc, vc = adamw_update(weight_chan, moment_chan, second_chan, mean_c, clip_factor)
    we, me, ve = adamw_update(weight_embed, moment_embed, second_embed, mean_e, clip_factor)
    gathered = (
        lax.all_gather(wx.astype(jnp.bfloat16), "shard", axis=1, tiled=True),
        lax.all_gather(wc.astype(jnp.bfloat16), "shard", axis=2, tiled=True),
        lax.all_gather(we.astype(jnp.bfloat16), "shard", axis=0, tiled=True),
    )
    return (
        wx,
        wc,
        we,
        mx,
        mc,
        me,
        vx,
        vc,
        ve,
        gathered[0],
        gathered[1],
        gathered[2],
        jnp.reshape(norm_value, (1,)),
    )


def solution(mesh):
    placed = (
        P(("rep", "shard"), None, None, None),
        P(("rep", "shard"), None, None, None),
        P(("rep", "shard"), None, None),
        P(None, "shard", None),
        P(None, None, "shard"),
        P("shard", None),
        P(None, "shard", None),
        P(None, None, "shard"),
        P("shard", None),
        P(None, "shard", None),
        P(None, None, "shard"),
        P("shard", None),
    )
    return jax.shard_map(
        on_device,
        mesh=mesh,
        in_specs=placed,
        out_specs=(
            P(None, "shard", None),
            P(None, None, "shard"),
            P("shard", None),
            P(None, "shard", None),
            P(None, None, "shard"),
            P("shard", None),
            P(None, "shard", None),
            P(None, None, "shard"),
            P("shard", None),
            P(),
            P(),
            P(),
            P(),
        ),
        check_vma=False,
    )
```

profile of v0, /device:TPU:1, one launch (start us, length us, event | category | flops | bytes accessed | tf_op | source)
XLA Modules:
  0.0 956.5 jit_solution(9110890464267347480)
XLA Ops:
  7.2 0.0 all-reduce.9.cloned.1.call-start
  7.2 6.5 reduce_sum.65
  13.7 1.0 reshape.52
  14.7 2.2 copy.42
  16.9 4.0 reduce_sum.63
  20.9 0.0 all-reduce.9.cloned.1.call-update
  20.9 0.0 reduce-scatter.5.cloned.1.call-start
  21.0 6.5 reduce_sum.67
  27.5 0.0 reduce-scatter.5.cloned.1.call-update
  27.5 0.0 all-reduce.7.cloned.1.call-start
  27.6 0.6 copy-done.6
  28.1 0.6 dynamic-slice
  28.7 85.4 %all-reduce.9.cloned.1.call-done = (bf16[2,2,1536,128]{3,2,0,1:T(8,128)(2,1)}, bf16[2,2,118,1536]{3,1,2,0:T(2,128)(2,1)}) async-done(((bf16[2,2,1536,128]{3,2,0,1:T(8,128)(2,1)}, bf16[2,2,118,1536]{3,1,2,0:T(2,128)(2,1)}), (bf16[2,2,1536,128]{3,2,0,1:T(8,128)(2,1)}, bf16[2,2,118,1536]{3,1,2,0:T(2,128)(2,1)})) %all-reduce.9.cloned.1.call-update) | async-done | bytes 3022864
  114.2 2.4 constant_dynamic-slice_fusion
  116.5 0.9 copy.43
  117.5 0.0 copy-done.5
  117.5 1.6 constant_dynamic-slice_fusion.1
  119.1 45.0 %reduce-scatter.5.cloned.1.call-done = bf16[512,1536]{1,0:T(8,128)(2,1)} async-done(((bf16[1024,1536]{1,0:T(8,128)(2,1)}), bf16[512,1536]{1,0:T(8,128)(2,1)}) %reduce-scatter.5.cloned.1.call-update) | async-done | bytes 1572880 | tf_op jit(solution)/shard_map/reduce_scatter | solution.py:53
  164.1 0.0 all-reduce.7.cloned.1.call-update
  164.1 0.2 all-gather.6.cloned.1.call-start
  164.3 647.6 %all-reduce.7.cloned.1.call-done = (bf16[1,2,1536,128]{3,2,0,1:T(8,128)(2,1)}, bf16[1,2,118,1536]{3,2,1,0:T(8,128)(2,1)}, bf16[512,1536]{1,0:T(8,128)(2,1)}) async-done(((bf16[1,2,1536,128]{3,2,0,1:T(8,128)(2,1)}, bf16[1,2,118,1536]{3,2,1,0:T(8,128)(2,1)}, bf16[512,1536]{1,0:T(8,128)(2,1)}), (bf16[1,2,1536,128]{3,2,0,1:T(8,128)(2,1)}, bf16[1,2,118,1536]{3,2,1,0:T(8,128)(2,1)}, ...) | async-done | bytes 3084304 | tf_op jit(solution)/shard_map/psum | solution.py:56
  812.0 2.2 fusion.12
  814.1 2.1 fusion.6
  816.3 2.8 fusion.3
  821.0 4.3 psum.31
  826.1 0.0 copy-done.4
  826.1 5.5 fusion.20
  831.6 0.0 all-gather.6.cloned.1.call-update
  831.6 0.0 all-gather.4.cloned.1.call-start
  831.7 0.0 copy-start
  831.7 6.0 fusion.23
  837.7 0.0 all-gather.4.cloned.1.call-update
  837.8 0.0 all-gather.8.cloned.1.call-start
  837.8 0.0 copy-done
  837.8 7.3 fusion.17
  845.1 0.0 all-gather.8.cloned.1.call-update
  845.1 0.0 copy-start.1
  845.2 1.3 copy-done.2
  846.5 2.2 copy.48
  848.7 0.0 copy-done.1
  848.7 2.2 copy.49
  850.9 2.2 copy.50
  853.2 8.0 all-gather.6.cloned.1.call-done
  861.1 4.0 copy.51
  865.1 28.4 %all-gather.4.cloned.1.call-done = bf16[2,3072,128]{2,1,0:T(8,128)(2,1)} async-done(((bf16[2,1536,128]{2,1,0:T(8,128)(2,1)}), bf16[2,3072,128]{2,1,0:T(8,128)(2,1)}) %all-gather.4.cloned.1.call-update) | async-done | bytes 1572880 | tf_op jit(solution)/shard_map/all_gather | solution.py:71
  893.4 50.6 %all-gather.8.cloned.1.call-done = bf16[1024,1536]{1,0:T(8,128)(2,1)} async-done(((bf16[512,1536]{1,0:T(8,128)(2,1)}), bf16[1024,1536]{1,0:T(8,128)(2,1)}) %all-gather.8.cloned.1.call-update) | async-done | bytes 3145744 | tf_op jit(solution)/shard_map/all_gather | solution.py:73
  944.1 2.8 copy.73
  946.9 1.7 copy.74
  (6 shorter events, 0.0 us)
Async XLA Ops:
  7.2 107.0 %all-reduce.9.cloned.1.call-start = ((), (), s32[]{:S(2)}) async-start(), calls=%async_computation.6 | async-start | bytes 6045696
  20.9 143.1 %reduce-scatter.5.cloned.1.call-start = ((), (), s32[]{:S(2)}) async-start(), calls=%async_computation.1 | async-start | bytes 4718592 | tf_op jit(solution)/shard_map/reduce_scatter | solution.py:53
  27.5 0.7 copy-start.6
  27.5 784.4 %all-reduce.7.cloned.1.call-start = ((), (), s32[]{:S(2)}) async-start(), calls=%async_computation.5 | async-start | bytes 6193152 | tf_op jit(solution)/shard_map/psum | solution.py:56
  114.1 3.3 copy-start.5
  164.1 697.0 %all-gather.6.cloned.1.call-start = ((), (), s32[]{:S(2)}) async-start(), calls=%async_computation.3 | async-start | bytes 2211840 | tf_op jit(solution)/shard_map/all_gather | solution.py:72
  811.9 14.1 %copy-start.4 = (bf16[1,2,118,1536]{3,2,1,0:T(8,128)(2,1)S(1)}, bf16[1,2,118,1536]{3,2,1,0:T(8,128)(2,1)}, u32[]{:S(2)}) copy-start(bf16[1,2,118,1536]{3,2,1,0:T(8,128)(2,1)} %get-tuple-element.53) | copy-start | bytes 2174980
  831.6 61.8 %all-gather.4.cloned.1.call-start = ((), (), s32[]{:S(2)}) async-start(), calls=%async_computation.2 | async-start | bytes 2359296 | tf_op jit(solution)/shard_map/all_gather | solution.py:71
  831.7 6.1 copy-start
  837.8 106.3 %all-gather.8.cloned.1.call-start = ((), (), s32[]{:S(2)}) async-start(), calls=%async_computation.4 | async-start | bytes 4718592 | tf_op jit(solution)/shard_map/all_gather | solution.py:73
  845.1 1.4 copy-start.2
  845.1 3.6 copy-start.1
  944.1 2.8 copy-start.3
Sparse Core Ops, SparseCore 0:
  21.1 93.0 all-reduce.8
  117.2 46.8 reduce-scatter.4
  167.9 643.9 all-reduce.6
  831.8 29.3 all-gather.5
  862.7 30.6 all-gather.3
  895.6 48.4 all-gather.7
where the time goes:
time: 957 us
  waiting for transfers between devices  865 us (90%)
  other arithmetic  43 us (4%)
  local copies, waits for them, and re-layouts  25.7 us (3%)
  between operations  18 us (2%)
    psum x1, waiting for transfers between devices, on_device(): block_x = lax.psum(part_x, 'rep')[0]  648 us
    unnamed x7, waiting for transfers between devices  85.5 us
    all_gather x1, waiting for transfers between devices, on_device(): lax.all_gather(we.astype(jnp.bfloat16), 'shard', axis=0, tiled=True)  50.6 us
    reduce_scatter x1, waiting for transfers between devices, on_device(): lax.psum_scatter(summed_e.astype(jnp.bfloat16), 'shard', scatter_dimensio...  45 us
    all_gather x1, waiting for transfers between devices, on_device(): lax.all_gather(wx.astype(jnp.bfloat16), 'shard', axis=1, tiled=True)  28.4 us
    unnamed x23, local copies, waits for them, and re-layouts  21.6 us
  transfers between devices with their start and end apart: 6, of which 6 were waited for; matrix products, arithmetic and copies ran while one was open for 4% of the time, Pallas kernels for 0%

commit v1 on v0

--- a/solution.py
+++ b/solution.py
@@ -53,7 +53,7 @@
     part_e = lax.psum_scatter(
         summed_e.astype(jnp.bfloat16), "shard", scatter_dimension=0, tiled=True
     )
-    block_x = lax.psum(part_x, "rep")[0]
+    block_x = jnp.sum(lax.all_gather(part_x, "rep"), axis=0)[0]
     block_c = lax.psum(part_c, "rep")[0]
     block_e = lax.psum(part_e, "rep")
     inverse = 1.0 / (micro * count_rep * count_shard)

time: 957 us -> 1170 us (1.22)
  waiting for transfers between devices: 865 us -> 1060 us
  other arithmetic: 43 us -> 58.3 us
    all_gather x0 -> x1, waiting for transfers between devices: none -> 210 us  [on_device(): block_x = jnp.sum(lax.all_gather(part_x, 'rep'), axis=0)[0]]
    reduce_sum x0 -> x1, other arithmetic: none -> 16.3 us  [on_device(): block_x = jnp.sum(lax.all_gather(part_x, 'rep'), axis=0)[0]]
    psum x1, waiting for transfers between devices: 648 us -> 634 us  [on_device(): block_c = lax.psum(part_c, 'rep')[0]]
    unnamed x7 -> x8, waiting for transfers between devices: 85.5 us -> 85.5 us
  transfers between devices with their start and end apart: 6 -> 7, of which waited for: 6 -> 7; matrix products, arithmetic and copies ran while one was open for 4% -> 4% of each run, Pallas kernels for 0% -> 0%
where the time goes in v1:
time: 1170 us
  waiting for transfers between devices  1060 us (91%)
  other arithmetic  58.3 us (5%)
  local copies, waits for them, and re-layouts  25.6 us (2%)
  between operations  18 us (2%)
    psum x1, waiting for transfers between devices, on_device(): block_c = lax.psum(part_c, 'rep')[0]  634 us
    all_gather x1, waiting for transfers between devices, on_device(): block_x = jnp.sum(lax.all_gather(part_x, 'rep'), axis=0)[0]  210 us
    unnamed x8, waiting for transfers between devices  85.5 us
    all_gather x1, waiting for transfers between devices, on_device(): lax.all_gather(we.astype(jnp.bfloat16), 'shard', axis=0, tiled=True)  50.8 us
    reduce_scatter x1, waiting for transfers between devices, on_device(): lax.psum_scatter(summed_e.astype(jnp.bfloat16), 'shard', scatter_dimensio...  46.7 us
    all_gather x1, waiting for transfers between devices, on_device(): lax.all_gather(wx.astype(jnp.bfloat16), 'shard', axis=1, tiled=True)  28.4 us
  transfers between devices with their start and end apart: 7, of which 7 were waited for; matrix products, arithmetic and copies ran while one was open for 4% of the time, Pallas kernels for 0%

profile of v1, /device:TPU:1, one launch (start us, length us, event | category | flops | bytes accessed | tf_op | source)
XLA Modules:
  0.0 1167.4 jit_solution(2826126833627851653)
XLA Ops:
  7.2 0.0 all-reduce.9.cloned.1.call-start
  7.2 6.5 reduce_sum.78
  13.7 1.0 reshape.50
  14.7 2.2 copy.42
  16.9 4.0 reduce_sum.75
  20.9 0.0 all-reduce.9.cloned.1.call-update
  20.9 0.0 reduce-scatter.5.cloned.1.call-start
  21.0 6.5 reduce_sum.80
  27.5 0.0 reduce-scatter.5.cloned.1.call-update
  27.5 0.0 all-reduce.7.cloned.1.call-start
  27.6 0.6 copy-done.8
  28.1 0.6 dynamic-slice
  28.7 85.4 %all-reduce.9.cloned.1.call-done = (bf16[2,2,1536,128]{3,2,0,1:T(8,128)(2,1)}, bf16[2,2,118,1536]{3,1,2,0:T(2,128)(2,1)}) async-done(((bf16[2,2,1536,128]{3,2,0,1:T(8,128)(2,1)}, bf16[2,2,118,1536]{3,1,2,0:T(2,128)(2,1)}), (bf16[2,2,1536,128]{3,2,0,1:T(8,128)(2,1)}, bf16[2,2,118,1536]{3,1,2,0:T(2,128)(2,1)})) %all-reduce.9.cloned.1.call-update) | async-done | bytes 3022864
  114.1 2.3 constant_dynamic-slice_fusion
  116.4 0.0 copy-start.7
  116.4 0.9 copy.43
  117.4 46.7 %reduce-scatter.5.cloned.1.call-done = bf16[512,1536]{1,0:T(8,128)(2,1)} async-done(((bf16[1024,1536]{1,0:T(8,128)(2,1)}), bf16[512,1536]{1,0:T(8,128)(2,1)}) %reduce-scatter.5.cloned.1.call-update) | async-done | bytes 1572880 | tf_op jit(solution)/shard_map/reduce_scatter | solution.py:53
  164.1 0.0 all-reduce.7.cloned.1.call-update
  164.1 0.0 all-gather.12.cloned.1.call-start
  164.1 0.0 copy-done.7
  164.1 1.6 constant_dynamic-slice_fusion.1
  165.7 0.0 all-gather.12.cloned.1.call-update
  165.8 0.2 all-gather.8.cloned.1.call-start
  166.0 633.7 %all-reduce.7.cloned.1.call-done = (bf16[1,2,118,1536]{3,2,1,0:T(8,128)(2,1)}, bf16[512,1536]{1,0:T(8,128)(2,1)}) async-done(((bf16[1,2,118,1536]{3,2,1,0:T(8,128)(2,1)}, bf16[512,1536]{1,0:T(8,128)(2,1)}), (bf16[1,2,118,1536]{3,2,1,0:T(8,128)(2,1)}, bf16[512,1536]{1,0:T(8,128)(2,1)})) %all-reduce.7.cloned.1.call-update) | async-done | bytes 2297872 | tf_op jit(solution)/shard_map/psum | solution.py:57
  799.7 2.1 fusion.11
  801.8 2.8 fusion.3
  804.6 210.5 %all-gather.12.cloned.1.call-done = bf16[64,2,1536,128]{3,2,0,1:T(8,128)(2,1)} async-done(((bf16[1,2,1536,128]{3,2,0,1:T(8,128)(2,1)}), bf16[64,2,1536,128]{3,2,0,1:T(8,128)(2,1)}) %all-gather.12.cloned.1.call-update) | async-done | bytes 50331664 | tf_op jit(solution)/shard_map/all_gather | solution.py:56
  1015.1 16.3 %reduce.8 = bf16[2,1536,128]{2,1,0:T(8,128)(2,1)S(1)} reduce(bf16[64,2,1536,128]{3,2,0,1:T(8,128)(2,1)} %all-gather.12.cloned.1.call-done, bf16[]{:T(256)} %constant.14.clone.1), dimensions={0}, to_apply=%region_2.0 | reduce | flops 24772608 | bytes 51118080 | tf_op jit(solution)/shard_map/reduce_sum | solution.py:56
  1031.4 1.0 fusion.8
  1034.4 4.3 psum.23
  1039.4 5.3 fusion.19
  1044.7 0.0 all-gather.8.cloned.1.call-update
  1044.7 0.0 all-gather.6.cloned.1.call-start
  1044.8 5.8 fusion.22
  1050.6 0.0 all-gather.6.cloned.1.call-update
  1050.6 0.0 all-gather.10.cloned.1.call-start
  1050.6 8.0 fusion.16
  1058.7 0.0 all-gather.10.cloned.1.call-update
  1058.7 1.3 copy-done.3
  1060.1 2.2 copy.48
  1062.3 2.2 copy.49
  1064.5 2.2 copy.50
  1066.7 5.1 all-gather.8.cloned.1.call-done
  1071.8 4.0 copy.51
  1075.8 28.4 %all-gather.6.cloned.1.call-done = bf16[2,3072,128]{2,1,0:T(8,128)(2,1)} async-done(((bf16[2,1536,128]{2,1,0:T(8,128)(2,1)}), bf16[2,3072,128]{2,1,0:T(8,128)(2,1)}) %all-gather.6.cloned.1.call-update) | async-done | bytes 1572880 | tf_op jit(solution)/shard_map/all_gather | solution.py:71
  1104.2 50.8 %all-gather.10.cloned.1.call-done = bf16[1024,1536]{1,0:T(8,128)(2,1)} async-done(((bf16[512,1536]{1,0:T(8,128)(2,1)}), bf16[1024,1536]{1,0:T(8,128)(2,1)}) %all-gather.10.cloned.1.call-update) | async-done | bytes 3145744 | tf_op jit(solution)/shard_map/all_gather | solution.py:73
  1154.9 2.8 copy.72
  1157.7 1.7 copy.73
  (14 shorter events, 0.0 us)
Async XLA Ops:
  7.2 107.0 %all-reduce.9.cloned.1.call-start = ((), (), s32[]{:S(2)}) async-start(), calls=%async_computation.7 | async-start | bytes 6045696
  20.9 143.1 %reduce-scatter.5.cloned.1.call-start = ((), (), s32[]{:S(2)}) async-start(), calls=%async_computation.1 | async-start | bytes 4718592 | tf_op jit(solution)/shard_map/reduce_scatter | solution.py:53
  27.5 0.7 copy-start.8
  27.5 772.2 %all-reduce.7.cloned.1.call-start = ((), (), s32[]{:S(2)}) async-start(), calls=%async_computation.6 | async-start | bytes 4620288 | tf_op jit(solution)/shard_map/psum | solution.py:57
  116.4 47.7 %copy-start.7 = (bf16[2,2,1536,128]{3,2,0,1:T(8,128)(2,1)S(1)}, bf16[2,2,1536,128]{3,2,0,1:T(8,128)(2,1)}, u32[]{:S(2)}) copy-start(bf16[2,2,1536,128]{3,2,0,1:T(8,128)(2,1)} %get-tuple-element.54) | copy-start | bytes 4718596
  164.1 851.0 %all-gather.12.cloned.1.call-start = ((), (), s32[]{:S(2)}) async-start(), calls=%async_computation.5 | async-start | bytes 51118080 | tf_op jit(solution)/shard_map/all_gather | solution.py:56
  165.8 906.1 %all-gather.8.cloned.1.call-start = ((), (), s32[]{:S(2)}) async-start(), calls=%async_computation.3 | async-start | bytes 2211840 | tf_op jit(solution)/shard_map/all_gather | solution.py:72
  804.6 234.8 %copy-start.5 = (bf16[1,2,118,1536]{3,2,1,0:T(8,128)(2,1)S(1)}, bf16[1,2,118,1536]{3,2,1,0:T(8,128)(2,1)}, u32[]{:S(2)}) copy-start(bf16[1,2,118,1536]{3,2,1,0:T(8,128)(2,1)} %get-tuple-element.52) | copy-start | bytes 2174980
  1015.1 24.3 %copy-start.6 = (f32[2,118,1536]{2,0,1:T(2,128)S(1)}, f32[2,118,1536]{2,0,1:T(2,128)}, u32[]{:S(2)}) copy-start(f32[2,118,1536]{2,0,1:T(2,128)} %param.16) | copy-start | bytes 4349956
  1044.7 59.4 %all-gather.6.cloned.1.call-start = ((), (), s32[]{:S(2)}) async-start(), calls=%async_computation.2 | async-start | bytes 2359296 | tf_op jit(solution)/shard_map/all_gather | solution.py:71
  1044.8 5.9 copy-start
  1050.6 104.4 %all-gather.10.cloned.1.call-start = ((), (), s32[]{:S(2)}) async-start(), calls=%async_computation.4 | async-start | bytes 4718592 | tf_op jit(solution)/shard_map/all_gather | solution.py:73
  1058.7 1.4 copy-start.3
  1058.7 3.6 copy-start.2
  1062.3 2.2 copy-start.1
  1154.9 2.8 copy-start.4
Sparse Core Ops, SparseCore 0:
  21.1 93.0 all-reduce.8
  117.2 46.8 reduce-scatter.4
  167.2 632.4 all-reduce.6
  804.1 210.9 all-gather.11
  1044.9 26.9 all-gather.7
  1073.4 30.6 all-gather.5
  1106.5 48.4 all-gather.9
